TPU v7x, 32 devices: a whole 2x2x4 slice. The times are simulated.
32 devices in a mesh: dp: 4 (over z), pipe: 2 (over core), expert: 4 (over y, x).
Axes of the slice: x: 2, y: 2, z: 4, core: 2. Of those that a mesh axis runs over, the one named last changes fastest.
Arguments:
- tokens: bfloat16 [2, 96, 3072], P(None, 'expert'), may hold values from -6 to 6
- expert_ids: int32 [2, 2, 96, 2], P('pipe', None, 'expert'), may hold values from 0 to 3, all different within a row; in each aligned block of 24 rows (0 to 23, 24 to 47, ..., all dimensions but the last counted through in order) at most 16 rows name the same one
- gates: float32 [2, 2, 96, 2], P('pipe', None, 'expert'), may hold values from 0.1 to 1
- w_gate: bfloat16 [2, 4, 3072, 704], P('pipe', 'expert', None, 'dp'), may hold values from -0.109375 to 0.109375
- w_up: bfloat16 [2, 4, 3072, 704], P('pipe', 'expert', None, 'dp'), may hold values from -0.109375 to 0.109375
- w_down: bfloat16 [2, 4, 704, 3072], P('pipe', 'expert', 'dp'), may hold values from -0.3125 to 0.3125
Outputs:
- layer_out: bfloat16 [2, 2, 96, 3072], P('pipe', None, 'expert', 'dp')
Inputs may be any that keep to these rules, and one draw needn't show every extreme that they name: `expert_ids`: each token names 2 different experts in each layer. Among the tokens of one index of expert in one layer and micro-batch (aligned blocks of 24 tokens) no expert is named by more than 16 tokens, and in some block an expert is named by exactly 16.
All inputs are finite; a program needn't handle non-finite values.
Results may differ from a plain program's by a relative error of at most 0.0052.
Values may be sent and summed in bfloat16 or wider, within the bound.
No kernel may reach another device: no remote copies, remote signals or barrier semaphores. Data moves between devices by JAX's collectives and lax.ppermute only.
A program may use at most 64 MiB of HBM per device.

v0:
```python
import jax
import jax.numpy as jnp
from jax import lax
from jax.sharding import PartitionSpec as P

TOP = 2
CAP = 16
AXES = ("dp", "pipe", "expert")
SMALL_GROUP = 8


class Ring:

    def __init__(self, n):
        self.n = n
        self.xor = n & n - 1 == 0

    def ahead(self, me, s):
        return me ^ s if self.xor else (me + s) % self.n

    def behind(self, me, s):
        return me ^ s if self.xor else (me - s) % self.n

    def place(self, target, me):
        return target ^ me if self.xor else (target - me) % self.n


def build_maps(route_ids, route_gates, ring, me, rows_all):
    experts = ring.n
    flat_ids = route_ids.reshape(-1)
    onehot = (flat_ids[:, None] == jnp.arange(experts, dtype=jnp.int32)[None, :]).astype(jnp.int32)
    before = jnp.cumsum(onehot, axis=0) - onehot
    slot = jnp.sum(before * onehot, axis=1)
    placed = ring.place(flat_ids, me) * CAP + slot
    matches = jnp.arange(rows_all, dtype=jnp.int32)[:, None] == placed[None, :]
    dispatch_map = jnp.sum(matches.astype(jnp.float32).reshape(rows_all, -1, TOP), axis=2).astype(
        jnp.bfloat16
    )
    combine_map = jnp.sum(
        jnp.where(matches, route_gates.reshape(-1)[None, :], 0.0).reshape(rows_all, -1, TOP), axis=2
    )
    return (dispatch_map, combine_map)


def per_device(tokens, expert_ids, gates, w_gate, w_up, w_down):
    n_dp = lax.axis_size("dp")
    n_pipe = lax.axis_size("pipe")
    n_exp = lax.axis_size("expert")
    micro, tok_rows, width = tokens.shape
    units = w_gate.shape[3]
    columns = width // n_dp
    rows_all = n_exp * CAP
    d_me = lax.axis_index("dp")
    p_me = lax.axis_index("pipe")
    e_me = lax.axis_index("expert")
    dring = Ring(n_dp)
    ering = Ring(n_exp)
    small_dp = n_dp <= SMALL_GROUP

    def lin(d, p, e):
        return (d * n_pipe + p) * n_exp + e

    def expert_pairs(p, s, back):
        step = ering.behind if back else ering.ahead
        return [(lin(d, p, e), lin(d, p, step(e, s))) for d in range(n_dp) for e in range(n_exp)]

    def dp_pairs(p, s):
        return [
            (lin(d, p, e), lin(dring.ahead(d, s), p, e)) for d in range(n_dp) for e in range(n_exp)
        ]

    gate_local = w_gate[0, 0]
    up_local = w_up[0, 0]
    down_local = w_down[0, 0]
    if small_dp:
        down_parts = []
        for s in range(n_dp):
            piece = lax.dynamic_slice_in_dim(down_local, dring.ahead(d_me, s) * columns, columns, 1)
            down_parts.append(piece)
        down_parts, tokens = lax.optimization_barrier((down_parts, tokens))
        for s in range(1, n_dp):
            down_parts[s] = lax.ppermute(
                down_parts[s], "dp", [(i, dring.ahead(i, s)) for i in range(n_dp)]
            )
        down_full = jnp.concatenate(down_parts, axis=0)
    else:
        down_full = lax.all_to_all(down_local, "dp", 1, 0, tiled=True)
    route_ids = expert_ids[0]
    route_gates = gates[0]
    maps = [build_maps(route_ids[m], route_gates[m], ering, e_me, rows_all) for m in range(micro)]
    dispatch_map = jnp.stack([mp[0] for mp in maps])
    combine_map = jnp.stack([mp[1] for mp in maps])
    if ering.xor:
        combine_map = jnp.stack(
            [build_maps(route_ids[m], route_gates[m], ering, 0, rows_all)[1] for m in range(micro)]
        )

    def layer(current, p):
        outgoing = jnp.einsum(
            "mrt,mtd->mrd", dispatch_map, current, preferred_element_type=jnp.float32
        )
        outgoing = outgoing.astype(jnp.bfloat16).reshape(micro, n_exp, CAP, width)
        arrived = [outgoing[:, 0]]
        for s in range(1, n_exp):
            arrived.append(lax.ppermute(outgoing[:, s], AXES, expert_pairs(p, s, False)))
        flat_rows = jnp.stack(arrived, axis=1).reshape(-1, width)
        squares = jnp.mean(jnp.square(flat_rows.astype(jnp.float32)), axis=1, keepdims=True)
        inv_rms = lax.rsqrt(squares + 1e-05)
        gate_act = jnp.dot(flat_rows, gate_local, preferred_element_type=jnp.float32) * inv_rms
        up_act = jnp.dot(flat_rows, up_local, preferred_element_type=jnp.float32) * inv_rms
        hidden = (jax.nn.silu(gate_act) * up_act).astype(jnp.bfloat16)
        if small_dp:
            spread = jnp.broadcast_to(hidden[None], (n_dp,) + hidden.shape)
            gathered = lax.all_to_all(spread, "dp", 0, 0, tiled=True)
            order = jnp.stack([dring.behind(d_me, s) for s in range(n_dp)])
            gathered = jnp.take(gathered, order, axis=0)
            hidden_full = jnp.transpose(gathered, (1, 0, 2)).reshape(hidden.shape[0], n_dp * units)
        else:
            hidden_full = lax.all_gather(hidden, "dp", axis=1, tiled=True)
        expert_out = jnp.dot(hidden_full, down_full, preferred_element_type=jnp.float32).astype(
            jnp.bfloat16
        )
        expert_out = expert_out.reshape(micro, n_exp, CAP, columns)
        if ering.xor:
            order = jnp.stack([ering.place(j, e_me) for j in range(n_exp)])
            by_block = jnp.take(expert_out, order, axis=1)
            returned = lax.all_to_all(by_block, "expert", 1, 1, tiled=True).reshape(
                micro, rows_all, columns
            )
        else:
            returned = [expert_out[:, 0]]
            for s in range(1, n_exp):
                returned.append(lax.ppermute(expert_out[:, s], AXES, expert_pairs(p, s, True)))
            returned = jnp.stack(returned, axis=1).reshape(micro, rows_all, columns)
        mixed = jnp.einsum(
            "mrt,mrc->mtc",
            combine_map,
            returned.astype(jnp.float32),
            precision=lax.Precision.HIGHEST,
            preferred_element_type=jnp.float32,
        )
        current_cols = lax.dynamic_slice_in_dim(current, d_me * columns, columns, 2)
        return (current_cols.astype(jnp.float32) + mixed).astype(jnp.bfloat16)

    current = tokens
    result = None
    for p in range(n_pipe):
        cols = layer(current, p)
        result = cols if result is None else jnp.where(p_me == p, cols, result)
        if p + 1 < n_pipe:
            if small_dp:
                parts = []
                for s in range(n_dp):
                    pairs = [
                        (lin(d, p, e), lin(dring.ahead(d, s), p + 1, e))
                        for d in range(n_dp)
                        for e in range(n_exp)
                    ]
                    parts.append(lax.ppermute(cols, AXES, pairs))
                stacked = jnp.stack(parts)
                order = jnp.stack([dring.place(d_me, k) for k in range(n_dp)])
                stacked = jnp.take(stacked, order, axis=0)
                current = jnp.transpose(stacked, (1, 2, 0, 3)).reshape(micro, tok_rows, width)
            else:
                full = lax.all_gather(cols, "dp", axis=2, tiled=True)
                current = lax.ppermute(full, "pipe", [(p, p + 1)])
    return result[None]


def solution(mesh):
    return jax.shard_map(
        per_device,
        mesh=mesh,
        in_specs=(
            P(None, "expert", None),
            P("pipe", None, "expert", None),
            P("pipe", None, "expert", None),
            P("pipe", "expert", None, "dp"),
            P("pipe", "expert", None, "dp"),
            P("pipe", "expert", "dp", None),
        ),
        out_specs=P("pipe", None, "expert", "dp"),
        check_vma=False,
    )
```

profile of v0, /device:TPU:1, one launch (start us, length us, event | category | flops | bytes accessed | tf_op | source)
XLA Modules:
  0.0 94.3 jit_solution(11994145500577898993)
XLA Ops:
  0.0 2.2 %dynamic-slice_bitcast_fusion = (bf16[176,768]{1,0:T(8,128)(2,1)}, bf16[176,768]{1,0:T(8,128)(2,1)}, bf16[176,768]{1,0:T(8,128)(2,1)S(1)}, bf16[176,768]{1,0:T(8,128)(2,1)}) fusion(bf16[1,1,176,3072]{3,2,1,0:T(8,128)(2,1)} %param.15, s32[]{:T(128)S(6)} %select_n.72, s32[]{:T(128)S(6)} %select_n.70, s32[]{:T(128)S(6)} %select_n.69, s32[]{:T(128)S(6)} %select_n.71), kind=kLoop, calls=%fused_computation.33 | loop fusion | bytes 2162704 | tf_op jit(solution)/shard_map/dynamic_slice | solution.py:78
  2.2 2.1 %collective-permute-start.3 = (bf16[176,768]{1,0:T(8,128)(2,1)}, bf16[176,768]{1,0:T(8,128)(2,1)}, u32[]{:S(2)}, u32[]{:S(2)}) collective-permute-start(bf16[176,768]{1,0:T(8,128)(2,1)} %get-tuple-element.14), channel_id=1, source_target_pairs={{0,8},{8,0},{16,24},{24,16},{1,9},{9,1},{17,25},{25,17},{2,10},{10... | collective-permute-start | bytes 811016 | tf_op jit(solution)/shard_map/ppermute | solution.py:82
  4.4 2.3 %collective-permute-start.4 = (bf16[176,768]{1,0:T(8,128)(2,1)}, bf16[176,768]{1,0:T(8,128)(2,1)}, u32[]{:S(2)}, u32[]{:S(2)}) collective-permute-start(bf16[176,768]{1,0:T(8,128)(2,1)} %get-tuple-element.15), channel_id=1, source_target_pairs={{0,16},{8,24},{16,0},{24,8},{1,17},{9,25},{17,1},{25,9},{2,18},{10... | collective-permute-start | bytes 811016 | tf_op jit(solution)/shard_map/ppermute | solution.py:82
  8.2 0.4 convolution_convert_fusion.1
  8.7 0.7 fusion.20
  9.4 1.3 %collective-permute-start = (bf16[2,16,3072]{2,1,0:T(8,128)(2,1)}, bf16[2,16,3072]{2,1,0:T(8,128)(2,1)}, u32[]{:S(2)}, u32[]{:S(2)}) collective-permute-start(bf16[2,16,3072]{2,1,0:T(8,128)(2,1)} %get-tuple-element.35), channel_id=1, source_target_pairs={{0,1},{1,0},{2,3},{3,2},{8,9},{9,8},{10,11},{11,10},{16,17},{17,16... | collective-permute-start | bytes 589832 | tf_op jit(solution)/shard_map/ppermute | solution.py:105
  10.7 1.4 %collective-permute-start.1 = (bf16[2,16,3072]{2,1,0:T(8,128)(2,1)S(1)}, bf16[2,16,3072]{2,1,0:T(8,128)(2,1)}, u32[]{:S(2)}, u32[]{:S(2)}) collective-permute-start(bf16[2,16,3072]{2,1,0:T(8,128)(2,1)S(1)} %get-tuple-element.34), channel_id=1, source_target_pairs={{0,2},{1,3},{2,0},{3,1},{8,10},{9,11},{10,8},{11,9},{16,18},{17,19... | collective-permute-start | bytes 589832 | tf_op jit(solution)/shard_map/ppermute | solution.py:105
  12.1 1.3 %collective-permute-start.2 = (bf16[2,16,3072]{2,1,0:T(8,128)(2,1)S(1)}, bf16[2,16,3072]{2,1,0:T(8,128)(2,1)}, u32[]{:S(2)}, u32[]{:S(2)}) collective-permute-start(bf16[2,16,3072]{2,1,0:T(8,128)(2,1)S(1)} %get-tuple-element.36), channel_id=1, source_target_pairs={{0,3},{1,2},{2,1},{3,0},{8,11},{9,10},{10,9},{11,8},{16,19},{17,18... | collective-permute-start | bytes 589832 | tf_op jit(solution)/shard_map/ppermute | solution.py:105
  13.8 1.3 %multiply_reduce_fusion.1 = (f32[2,4,16]{2,1,0:T(4,128)S(1)}, bf16[2,4,16,3072]{3,2,1,0:T(8,128)(2,1)S(1)}) fusion(bf16[2,1,16,3072]{3,2,1,0:T(8,128)(2,1)} %bitcast.28, bf16[2,1,16,3072]{3,2,1,0:T(8,128)(2,1)} %bitcast.26, bf16[2,1,16,3072]{3,2,1,0:T(8,128)(2,1)} %bitcast.24, bf16[2,1,16,3072]{3,2,1,0:T(8,128)(2,1)S(1)} %get-tuple-element.33), kind=kLoop, calls=%fused_computation.8 | loop fusion | flops 2359168 | bytes 1573376 | tf_op jit(solution)/shard_map/reduce_sum | solution.py:107
  15.3 0.4 convolution_multiply_fusion.3
  15.7 0.8 copy-done.1
  16.5 0.5 fusion.6
  17.0 0.7 broadcast_in_dim.85
  17.7 4.5 %all-to-all-start = ((bf16[4,128,176]{1,2,0:T(8,128)(2,1)}), bf16[4,128,176]{1,2,0:T(8,128)(2,1)S(1)}, u32[]{:S(2)}, u32[]{:S(2)}) async-start(bf16[4,128,176]{1,2,0:T(8,128)(2,1)} %broadcast_in_dim.85), calls=%async_computation | async-start | bytes 360448 | tf_op jit(solution)/shard_map/all_to_all | solution.py:114
  22.2 1.0 %constant_dynamic-update-slice_fusion.2 = bf16[704,768]{1,0:T(8,128)(2,1)S(1)} fusion(bf16[704,768]{1,0:T(8,128)(2,1)S(1)} %constant_dynamic-update-slice_fusion.3, bf16[176,768]{1,0:T(8,128)(2,1)} %collective-permute-done.3), kind=kLoop, calls=%fused_computation.65 | loop fusion | bytes 540672
  23.2 1.0 %constant_dynamic-update-slice_fusion.1 = bf16[704,768]{1,0:T(8,128)(2,1)S(1)} fusion(bf16[704,768]{1,0:T(8,128)(2,1)S(1)} %constant_dynamic-update-slice_fusion.2, bf16[176,768]{1,0:T(8,128)(2,1)} %collective-permute-done.4), kind=kLoop, calls=%fused_computation.64 | loop fusion | bytes 540672
  24.1 1.0 %constant_dynamic-update-slice_fusion = bf16[704,768]{1,0:T(8,128)(2,1)S(1)} fusion(bf16[704,768]{1,0:T(8,128)(2,1)S(1)} %constant_dynamic-update-slice_fusion.1, bf16[176,768]{1,0:T(8,128)(2,1)} %collective-permute-done.5), kind=kLoop, calls=%fused_computation.63 | loop fusion | bytes 540672 | tf_op jit(solution)/shard_map/concatenate | solution.py:85
  25.1 7.9 %all-to-all-done = bf16[4,128,176]{1,2,0:T(8,128)(2,1)S(1)} async-done(((bf16[4,128,176]{1,2,0:T(8,128)(2,1)}), bf16[4,128,176]{1,2,0:T(8,128)(2,1)S(1)}, u32[]{:S(2)}, u32[]{:S(2)}) %all-to-all-start) | async-done | bytes 180256 | tf_op jit(solution)/shard_map/all_to_all | solution.py:114
  33.0 0.6 gather_fusion.1
  34.1 0.6 gather_fusion.2
  34.7 0.8 select_bitcast_fusion.2
  35.5 3.4 %all-to-all-start.1 = ((bf16[2,4,16,768]{3,2,0,1:T(8,128)(2,1)}), bf16[2,4,16,768]{3,2,0,1:T(8,128)(2,1)S(1)}, u32[]{:S(2)}, u32[]{:S(2)}) async-start(bf16[2,4,16,768]{3,2,0,1:T(8,128)(2,1)} %select_bitcast_fusion.2), calls=%async_computation.1 | async-start | bytes 393216 | tf_op jit(solution)/shard_map/all_to_all | solution.py:127
  39.1 3.9 %all-to-all-done.1 = bf16[2,4,16,768]{3,2,0,1:T(8,128)(2,1)S(1)} async-done(((bf16[2,4,16,768]{3,2,0,1:T(8,128)(2,1)}), bf16[2,4,16,768]{3,2,0,1:T(8,128)(2,1)S(1)}, u32[]{:S(2)}, u32[]{:S(2)}) %all-to-all-start.1) | async-done | bytes 196640 | tf_op jit(solution)/shard_map/all_to_all | solution.py:127
  43.2 1.3 %collective-permute-start.6 = (bf16[2,24,768]{2,1,0:T(8,128)(2,1)S(1)}, bf16[2,24,768]{2,1,0:T(8,128)(2,1)S(1)}, u32[]{:S(2)}, u32[]{:S(2)}) collective-permute-start(bf16[2,24,768]{2,1,0:T(8,128)(2,1)S(1)} %fusion), channel_id=1, source_target_pairs={{0,4},{1,5},{2,6},{3,7},{8,12},{9,13},{10,14},{11,15},{16,20},{17,... | collective-permute-start | bytes 221192 | tf_op jit(solution)/shard_map/ppermute | solution.py:159
  44.5 1.3 %collective-permute-start.7 = (bf16[2,24,768]{2,1,0:T(8,128)(2,1)S(1)}, bf16[2,24,768]{2,1,0:T(8,128)(2,1)S(1)}, u32[]{:S(2)}, u32[]{:S(2)}) collective-permute-start(bf16[2,24,768]{2,1,0:T(8,128)(2,1)S(1)} %fusion), channel_id=1, source_target_pairs={{0,12},{1,13},{2,14},{3,15},{8,4},{9,5},{10,6},{11,7},{16,28},{17,... | collective-permute-start | bytes 221192 | tf_op jit(solution)/shard_map/ppermute | solution.py:159
  45.8 1.3 %collective-permute-start.8 = (bf16[2,24,768]{2,1,0:T(8,128)(2,1)S(1)}, bf16[2,24,768]{2,1,0:T(8,128)(2,1)S(1)}, u32[]{:S(2)}, u32[]{:S(2)}) collective-permute-start(bf16[2,24,768]{2,1,0:T(8,128)(2,1)S(1)} %fusion), channel_id=1, source_target_pairs={{0,20},{1,21},{2,22},{3,23},{8,28},{9,29},{10,30},{11,31},{16,4},{... | collective-permute-start | bytes 221192 | tf_op jit(solution)/shard_map/ppermute | solution.py:159
  47.1 1.3 %collective-permute-start.9 = (bf16[2,24,768]{2,1,0:T(8,128)(2,1)S(1)}, bf16[2,24,768]{2,1,0:T(8,128)(2,1)S(1)}, u32[]{:S(2)}, u32[]{:S(2)}) collective-permute-start(bf16[2,24,768]{2,1,0:T(8,128)(2,1)S(1)} %fusion), channel_id=1, source_target_pairs={{0,28},{1,29},{2,30},{3,31},{8,20},{9,21},{10,22},{11,23},{16,12},... | collective-permute-start | bytes 221192 | tf_op jit(solution)/shard_map/ppermute | solution.py:159
  48.4 4.2 %collective-permute-done.6 = bf16[2,24,768]{2,1,0:T(8,128)(2,1)S(1)} collective-permute-done((bf16[2,24,768]{2,1,0:T(8,128)(2,1)S(1)}, bf16[2,24,768]{2,1,0:T(8,128)(2,1)S(1)}, u32[]{:S(2)}, u32[]{:S(2)}) %collective-permute-start.6) | collective-permute-done | bytes 73760 | tf_op jit(solution)/shard_map/ppermute | solution.py:159
  52.6 3.6 %collective-permute-done.7 = bf16[2,24,768]{2,1,0:T(8,128)(2,1)S(1)} collective-permute-done((bf16[2,24,768]{2,1,0:T(8,128)(2,1)S(1)}, bf16[2,24,768]{2,1,0:T(8,128)(2,1)S(1)}, u32[]{:S(2)}, u32[]{:S(2)}) %collective-permute-start.7) | collective-permute-done | bytes 73760 | tf_op jit(solution)/shard_map/ppermute | solution.py:159
  56.2 0.8 collective-permute-done.8
  57.0 2.3 %collective-permute-done.9 = bf16[2,24,768]{2,1,0:T(8,128)(2,1)S(1)} collective-permute-done((bf16[2,24,768]{2,1,0:T(8,128)(2,1)S(1)}, bf16[2,24,768]{2,1,0:T(8,128)(2,1)S(1)}, u32[]{:S(2)}, u32[]{:S(2)}) %collective-permute-start.9) | collective-permute-done | bytes 73760 | tf_op jit(solution)/shard_map/ppermute | solution.py:159
  59.4 0.6 gather_fusion
  60.1 0.4 convolution_convert_fusion
  60.6 2.7 %collective-permute-start.10 = (bf16[2,16,3072]{2,1,0:T(8,128)(2,1)S(1)}, bf16[2,16,3072]{2,1,0:T(8,128)(2,1)S(1)}, u32[]{:S(2)}, u32[]{:S(2)}) collective-permute-start(bf16[2,16,3072]{2,1,0:T(8,128)(2,1)S(1)} %get-tuple-element.31), channel_id=1, source_target_pairs={{4,5},{5,4},{6,7},{7,6},{12,13},{13,12},{14,15},{15,14},{20,21},{2... | collective-permute-start | bytes 589832 | tf_op jit(solution)/shard_map/ppermute | solution.py:105
  63.3 2.2 %collective-permute-start.11 = (bf16[2,16,3072]{2,1,0:T(8,128)(2,1)S(1)}, bf16[2,16,3072]{2,1,0:T(8,128)(2,1)S(1)}, u32[]{:S(2)}, u32[]{:S(2)}) collective-permute-start(bf16[2,16,3072]{2,1,0:T(8,128)(2,1)S(1)} %get-tuple-element.30), channel_id=1, source_target_pairs={{4,6},{5,7},{6,4},{7,5},{12,14},{13,15},{14,12},{15,13},{20,22},{2... | collective-permute-start | bytes 589832 | tf_op jit(solution)/shard_map/ppermute | solution.py:105
  65.5 3.5 %collective-permute-start.12 = (bf16[2,16,3072]{2,1,0:T(8,128)(2,1)S(1)}, bf16[2,16,3072]{2,1,0:T(8,128)(2,1)S(1)}, u32[]{:S(2)}, u32[]{:S(2)}) collective-permute-start(bf16[2,16,3072]{2,1,0:T(8,128)(2,1)S(1)} %get-tuple-element.32), channel_id=1, source_target_pairs={{4,7},{5,6},{6,5},{7,4},{12,15},{13,14},{14,13},{15,12},{20,23},{2... | collective-permute-start | bytes 589832 | tf_op jit(solution)/shard_map/ppermute | solution.py:105
  69.0 1.0 %collective-permute-done.11 = bf16[2,16,3072]{2,1,0:T(8,128)(2,1)S(1)} collective-permute-done((bf16[2,16,3072]{2,1,0:T(8,128)(2,1)S(1)}, bf16[2,16,3072]{2,1,0:T(8,128)(2,1)S(1)}, u32[]{:S(2)}, u32[]{:S(2)}) %collective-permute-start.11) | collective-permute-done | bytes 196640 | tf_op jit(solution)/shard_map/ppermute | solution.py:105
  70.0 2.9 %collective-permute-done.12 = bf16[2,16,3072]{2,1,0:T(8,128)(2,1)S(1)} collective-permute-done((bf16[2,16,3072]{2,1,0:T(8,128)(2,1)S(1)}, bf16[2,16,3072]{2,1,0:T(8,128)(2,1)S(1)}, u32[]{:S(2)}, u32[]{:S(2)}) %collective-permute-start.12) | collective-permute-done | bytes 196640 | tf_op jit(solution)/shard_map/ppermute | solution.py:105
  73.3 0.5 convolution_multiply_fusion.1
  73.8 0.8 copy-done.2
  74.6 0.5 fusion.7
  75.1 8.3 %all_to_all.20 = bf16[4,128,176]{1,2,0:T(8,128)(2,1)S(1)} all-to-all(bf16[4,128,176]{1,2,0:T(8,128)(2,1)S(1)} %broadcast_in_dim.87), channel_id=1, replica_groups=mesh['dp'=4,'pipe'=2,'expert'=4] {'dp'}, dimensions={0} | all-to-all | bytes 360448 | tf_op jit(solution)/shard_map/all_to_all | solution.py:114
  83.4 0.7 gather_fusion.3
  84.6 0.7 gather_fusion.4
  85.3 0.8 select_bitcast_fusion.1
  86.1 3.4 %all-to-all-start.3 = ((bf16[2,4,16,768]{3,2,0,1:T(8,128)(2,1)}), bf16[2,4,16,768]{3,2,0,1:T(8,128)(2,1)S(1)}, u32[]{:S(2)}, u32[]{:S(2)}) async-start(bf16[2,4,16,768]{3,2,0,1:T(8,128)(2,1)} %select_bitcast_fusion.1), calls=%async_computation.3 | async-start | bytes 393216 | tf_op jit(solution)/shard_map/all_to_all | solution.py:127
  89.4 4.0 %all-to-all-done.3 = bf16[2,4,16,768]{3,2,0,1:T(8,128)(2,1)S(1)} async-done(((bf16[2,4,16,768]{3,2,0,1:T(8,128)(2,1)}), bf16[2,4,16,768]{3,2,0,1:T(8,128)(2,1)S(1)}, u32[]{:S(2)}, u32[]{:S(2)}) %all-to-all-start.3) | async-done | bytes 196640 | tf_op jit(solution)/shard_map/all_to_all | solution.py:127
  93.5 0.9 fusion.5
  (75 shorter events, 3.8 us)
Async XLA Ops:
  0.0 15.3 %copy-start = (bf16[1,1,3072,176]{2,3,1,0:T(8,128)(2,1)S(1)}, bf16[1,1,3072,176]{2,3,1,0:T(8,128)(2,1)}, u32[]{:S(2)}) copy-start(bf16[1,1,3072,176]{2,3,1,0:T(8,128)(2,1)} %param.13) | copy-start | bytes 3244036
  0.0 6.7 %copy-start.4 = (s32[1,2,24,2]{2,3,1,0:T(2,128)S(1)}, s32[1,2,24,2]{2,3,1,0:T(2,128)}, u32[]{:S(2)}) copy-start(s32[1,2,24,2]{2,3,1,0:T(2,128)} %param.11) | copy-start | bytes 1156
  0.0 8.2 %copy-start.3 = (bf16[2,24,3072]{2,1,0:T(8,128)(2,1)S(1)}, bf16[2,24,3072]{2,1,0:T(8,128)(2,1)}, u32[]{:S(2)}) copy-start(bf16[2,24,3072]{2,1,0:T(8,128)(2,1)} %param.10) | copy-start | bytes 884740
  2.2 19.9 %collective-permute-start.3 = (bf16[176,768]{1,0:T(8,128)(2,1)}, bf16[176,768]{1,0:T(8,128)(2,1)}, u32[]{:S(2)}, u32[]{:S(2)}) collective-permute-start(bf16[176,768]{1,0:T(8,128)(2,1)} %get-tuple-element.14), channel_id=1, source_target_pairs={{0,8},{8,0},{16,24},{24,16},{1,9},{9,1},{17,25},{25,17},{2,10},{10... | collective-permute-start | bytes 811016 | tf_op jit(solution)/shard_map/ppermute | solution.py:82
  4.4 18.8 %collective-permute-start.4 = (bf16[176,768]{1,0:T(8,128)(2,1)}, bf16[176,768]{1,0:T(8,128)(2,1)}, u32[]{:S(2)}, u32[]{:S(2)}) collective-permute-start(bf16[176,768]{1,0:T(8,128)(2,1)} %get-tuple-element.15), channel_id=1, source_target_pairs={{0,16},{8,24},{16,0},{24,8},{1,17},{9,25},{17,1},{25,9},{2,18},{10... | collective-permute-start | bytes 811016 | tf_op jit(solution)/shard_map/ppermute | solution.py:82
  8.6 5.0 %copy-start.12 = (f32[1,2,24,2]{2,3,1,0:T(2,128)S(1)}, f32[1,2,24,2]{2,3,1,0:T(2,128)}, u32[]{:S(2)}) copy-start(f32[1,2,24,2]{2,3,1,0:T(2,128)} %param.12) | copy-start | bytes 1156
  9.4 4.3 %collective-permute-start = (bf16[2,16,3072]{2,1,0:T(8,128)(2,1)}, bf16[2,16,3072]{2,1,0:T(8,128)(2,1)}, u32[]{:S(2)}, u32[]{:S(2)}) collective-permute-start(bf16[2,16,3072]{2,1,0:T(8,128)(2,1)} %get-tuple-element.35), channel_id=1, source_target_pairs={{0,1},{1,0},{2,3},{3,2},{8,9},{9,8},{10,11},{11,10},{16,17},{17,16... | collective-permute-start | bytes 589832 | tf_op jit(solution)/shard_map/ppermute | solution.py:105
  10.7 3.0 %collective-permute-start.1 = (bf16[2,16,3072]{2,1,0:T(8,128)(2,1)S(1)}, bf16[2,16,3072]{2,1,0:T(8,128)(2,1)}, u32[]{:S(2)}, u32[]{:S(2)}) collective-permute-start(bf16[2,16,3072]{2,1,0:T(8,128)(2,1)S(1)} %get-tuple-element.34), channel_id=1, source_target_pairs={{0,2},{1,3},{2,0},{3,1},{8,10},{9,11},{10,8},{11,9},{16,18},{17,19... | collective-permute-start | bytes 589832 | tf_op jit(solution)/shard_map/ppermute | solution.py:105
  12.1 1.7 %collective-permute-start.2 = (bf16[2,16,3072]{2,1,0:T(8,128)(2,1)S(1)}, bf16[2,16,3072]{2,1,0:T(8,128)(2,1)}, u32[]{:S(2)}, u32[]{:S(2)}) collective-permute-start(bf16[2,16,3072]{2,1,0:T(8,128)(2,1)S(1)} %get-tuple-element.36), channel_id=1, source_target_pairs={{0,3},{1,2},{2,1},{3,0},{8,11},{9,10},{10,9},{11,8},{16,19},{17,18... | collective-permute-start | bytes 589832 | tf_op jit(solution)/shard_map/ppermute | solution.py:105
  13.5 20.1 %copy-start.5 = (pred[4]{0:T(512)(128)(4,1)}, pred[4]{0:T(512)(128)(4,1)S(1)}, u32[]{:S(2)}) copy-start(pred[4]{0:T(512)(128)(4,1)S(1)} %get-tuple-element.21) | copy-start | bytes 16
  13.5 19.5 %copy-start.8 = (s32[1024]{0:T(1024)}, s32[1024]{0:T(1024)S(1)}, u32[]{:S(2)}) copy-start(s32[1024]{0:T(1024)S(1)} %pad_clamp_fusion.2) | copy-start | bytes 12292
  13.6 21.0 %copy-start.10 = (pred[4]{0:T(512)(128)(4,1)}, pred[4]{0:T(512)(128)(4,1)S(1)}, u32[]{:S(2)}) copy-start(pred[4]{0:T(512)(128)(4,1)S(1)} %get-tuple-element.19) | copy-start | bytes 16
  13.7 20.4 %copy-start.9 = (s32[1024]{0:T(1024)}, s32[1024]{0:T(1024)S(1)}, u32[]{:S(2)}) copy-start(s32[1024]{0:T(1024)S(1)} %pad_clamp_fusion.1) | copy-start | bytes 12292
  13.7 10.5 %collective-permute-start.5 = (bf16[176,768]{1,0:T(8,128)(2,1)}, bf16[176,768]{1,0:T(8,128)(2,1)}, u32[]{:S(2)}, u32[]{:S(2)}) collective-permute-start(bf16[176,768]{1,0:T(8,128)(2,1)} %get-tuple-element.16), channel_id=1, source_target_pairs={{0,24},{8,16},{16,8},{24,0},{1,25},{9,17},{17,9},{25,1},{2,26},{10... | collective-permute-start | bytes 811016 | tf_op jit(solution)/shard_map/ppermute | solution.py:82
  15.2 1.3 %copy-start.1 = (bf16[1,1,3072,176]{2,3,1,0:T(8,128)(2,1)S(1)}, bf16[1,1,3072,176]{2,3,1,0:T(8,128)(2,1)}, u32[]{:S(2)}) copy-start(bf16[1,1,3072,176]{2,3,1,0:T(8,128)(2,1)} %param.14) | copy-start | bytes 3244036
  17.7 15.4 %all-to-all-start = ((bf16[4,128,176]{1,2,0:T(8,128)(2,1)}), bf16[4,128,176]{1,2,0:T(8,128)(2,1)S(1)}, u32[]{:S(2)}, u32[]{:S(2)}) async-start(bf16[4,128,176]{1,2,0:T(8,128)(2,1)} %broadcast_in_dim.85), calls=%async_computation | async-start | bytes 360448 | tf_op jit(solution)/shard_map/all_to_all | solution.py:114
  35.5 7.5 %all-to-all-start.1 = ((bf16[2,4,16,768]{3,2,0,1:T(8,128)(2,1)}), bf16[2,4,16,768]{3,2,0,1:T(8,128)(2,1)S(1)}, u32[]{:S(2)}, u32[]{:S(2)}) async-start(bf16[2,4,16,768]{3,2,0,1:T(8,128)(2,1)} %select_bitcast_fusion.2), calls=%async_computation.1 | async-start | bytes 393216 | tf_op jit(solution)/shard_map/all_to_all | solution.py:127
  38.9 21.1 %copy-start.6 = (pred[4]{0:T(512)(128)(4,1)S(1)}, pred[4]{0:T(512)(128)(4,1)}, u32[]{:S(2)}) copy-start(pred[4]{0:T(512)(128)(4,1)} %copy-done.5) | copy-start | bytes 16
  43.2 9.4 %collective-permute-start.6 = (bf16[2,24,768]{2,1,0:T(8,128)(2,1)S(1)}, bf16[2,24,768]{2,1,0:T(8,128)(2,1)S(1)}, u32[]{:S(2)}, u32[]{:S(2)}) collective-permute-start(bf16[2,24,768]{2,1,0:T(8,128)(2,1)S(1)} %fusion), channel_id=1, source_target_pairs={{0,4},{1,5},{2,6},{3,7},{8,12},{9,13},{10,14},{11,15},{16,20},{17,... | collective-permute-start | bytes 221192 | tf_op jit(solution)/shard_map/ppermute | solution.py:159
  44.5 11.7 %collective-permute-start.7 = (bf16[2,24,768]{2,1,0:T(8,128)(2,1)S(1)}, bf16[2,24,768]{2,1,0:T(8,128)(2,1)S(1)}, u32[]{:S(2)}, u32[]{:S(2)}) collective-permute-start(bf16[2,24,768]{2,1,0:T(8,128)(2,1)S(1)} %fusion), channel_id=1, source_target_pairs={{0,12},{1,13},{2,14},{3,15},{8,4},{9,5},{10,6},{11,7},{16,28},{17,... | collective-permute-start | bytes 221192 | tf_op jit(solution)/shard_map/ppermute | solution.py:159
  45.8 11.3 %collective-permute-start.8 = (bf16[2,24,768]{2,1,0:T(8,128)(2,1)S(1)}, bf16[2,24,768]{2,1,0:T(8,128)(2,1)S(1)}, u32[]{:S(2)}, u32[]{:S(2)}) collective-permute-start(bf16[2,24,768]{2,1,0:T(8,128)(2,1)S(1)} %fusion), channel_id=1, source_target_pairs={{0,20},{1,21},{2,22},{3,23},{8,28},{9,29},{10,30},{11,31},{16,4},{... | collective-permute-start | bytes 221192 | tf_op jit(solution)/shard_map/ppermute | solution.py:159
  47.1 12.3 %collective-permute-start.9 = (bf16[2,24,768]{2,1,0:T(8,128)(2,1)S(1)}, bf16[2,24,768]{2,1,0:T(8,128)(2,1)S(1)}, u32[]{:S(2)}, u32[]{:S(2)}) collective-permute-start(bf16[2,24,768]{2,1,0:T(8,128)(2,1)S(1)} %fusion), channel_id=1, source_target_pairs={{0,28},{1,29},{2,30},{3,31},{8,20},{9,21},{10,22},{11,23},{16,12},... | collective-permute-start | bytes 221192 | tf_op jit(solution)/shard_map/ppermute | solution.py:159
  60.6 8.4 %collective-permute-start.10 = (bf16[2,16,3072]{2,1,0:T(8,128)(2,1)S(1)}, bf16[2,16,3072]{2,1,0:T(8,128)(2,1)S(1)}, u32[]{:S(2)}, u32[]{:S(2)}) collective-permute-start(bf16[2,16,3072]{2,1,0:T(8,128)(2,1)S(1)} %get-tuple-element.31), channel_id=1, source_target_pairs={{4,5},{5,4},{6,7},{7,6},{12,13},{13,12},{14,15},{15,14},{20,21},{2... | collective-permute-start | bytes 589832 | tf_op jit(solution)/shard_map/ppermute | solution.py:105
  63.3 6.7 %collective-permute-start.11 = (bf16[2,16,3072]{2,1,0:T(8,128)(2,1)S(1)}, bf16[2,16,3072]{2,1,0:T(8,128)(2,1)S(1)}, u32[]{:S(2)}, u32[]{:S(2)}) collective-permute-start(bf16[2,16,3072]{2,1,0:T(8,128)(2,1)S(1)} %get-tuple-element.30), channel_id=1, source_target_pairs={{4,6},{5,7},{6,4},{7,5},{12,14},{13,15},{14,12},{15,13},{20,22},{2... | collective-permute-start | bytes 589832 | tf_op jit(solution)/shard_map/ppermute | solution.py:105
  65.5 7.5 %collective-permute-start.12 = (bf16[2,16,3072]{2,1,0:T(8,128)(2,1)S(1)}, bf16[2,16,3072]{2,1,0:T(8,128)(2,1)S(1)}, u32[]{:S(2)}, u32[]{:S(2)}) collective-permute-start(bf16[2,16,3072]{2,1,0:T(8,128)(2,1)S(1)} %get-tuple-element.32), channel_id=1, source_target_pairs={{4,7},{5,6},{6,5},{7,4},{12,15},{13,14},{14,13},{15,12},{20,23},{2... | collective-permute-start | bytes 589832 | tf_op jit(solution)/shard_map/ppermute | solution.py:105
  73.3 1.3 %copy-start.2 = (bf16[1,1,3072,176]{2,3,1,0:T(8,128)(2,1)S(1)}, bf16[1,1,3072,176]{2,3,1,0:T(8,128)(2,1)}, u32[]{:S(2)}) copy-start(bf16[1,1,3072,176]{2,3,1,0:T(8,128)(2,1)} %param.14) | copy-start | bytes 3244036
  74.6 9.6 %copy-start.7 = (pred[4]{0:T(512)(128)(4,1)S(1)}, pred[4]{0:T(512)(128)(4,1)}, u32[]{:S(2)}) copy-start(pred[4]{0:T(512)(128)(4,1)} %copy-done.5) | copy-start | bytes 16
  84.1 1.1 %copy-start.11 = (pred[4]{0:T(512)(128)(4,1)S(1)}, pred[4]{0:T(512)(128)(4,1)}, u32[]{:S(2)}) copy-start(pred[4]{0:T(512)(128)(4,1)} %copy-done.10) | copy-start | bytes 16
  86.1 7.4 %all-to-all-start.3 = ((bf16[2,4,16,768]{3,2,0,1:T(8,128)(2,1)}), bf16[2,4,16,768]{3,2,0,1:T(8,128)(2,1)S(1)}, u32[]{:S(2)}, u32[]{:S(2)}) async-start(bf16[2,4,16,768]{3,2,0,1:T(8,128)(2,1)} %select_bitcast_fusion.1), calls=%async_computation.3 | async-start | bytes 393216 | tf_op jit(solution)/shard_map/all_to_all | solution.py:127
where the time goes:
time: 95.2 us; the launch traced here: 94.3 us
  starting transfers between devices  33.4 us (35%)
  waiting for transfers between devices  30.7 us (32%)
  local copies, waits for them, and re-layouts  12.3 us (13%)
  blocking collectives  8.35 us (9%)
  other arithmetic  4.58 us (5%)
  matrix products  4.44 us (5%)
    ppermute x6, starting transfers between devices, layer(): lax.ppermute(outgoing[:, s], AXES, expert_pairs(p, s, False))  12.4 us
    ppermute x4, waiting for transfers between devices, per_device(): parts.append(lax.ppermute(cols, AXES, pairs))  11 us
    all_to_all x1, blocking collectives, layer(): gathered = lax.all_to_all(spread, 'dp', 0, 0, tiled=True)  8.35 us
    all_to_all x1, waiting for transfers between devices, layer(): gathered = lax.all_to_all(spread, 'dp', 0, 0, tiled=True)  7.92 us
    all_to_all x2, waiting for transfers between devices, layer(): lax.all_to_all(by_block, 'expert', 1, 1, tiled=True)  7.88 us
    all_to_all x2, starting transfers between devices, layer(): lax.all_to_all(by_block, 'expert', 1, 1, tiled=True)  6.8 us
    ppermute x4, starting transfers between devices, per_device(): parts.append(lax.ppermute(cols, AXES, pairs))  5.17 us
    all_to_all x1, starting transfers between devices, layer(): gathered = lax.all_to_all(spread, 'dp', 0, 0, tiled=True)  4.51 us
  transfers between devices with their start and end apart: 16, of which 9 were waited for; matrix products, arithmetic and copies ran while one was open for 10% of the time, Pallas kernels for 0%

commit v1 on v0

--- a/solution.py
+++ b/solution.py
@@ -124,9 +124,12 @@
         if ering.xor:
             order = jnp.stack([ering.place(j, e_me) for j in range(n_exp)])
             by_block = jnp.take(expert_out, order, axis=1)
-            returned = lax.all_to_all(by_block, "expert", 1, 1, tiled=True).reshape(
-                micro, rows_all, columns
-            )
+            returned = jnp.concatenate(
+                lax.all_to_all(
+                    jnp.stack(jnp.split(by_block, lax.axis_size("expert"), axis=1)), "expert", 0, 0
+                ),
+                axis=1,
+            ).reshape(micro, rows_all, columns)
         else:
             returned = [expert_out[:, 0]]
             for s in range(1, n_exp):

time: 95.2 us -> 95.3 us (level)
    another operation x0 -> x2, other arithmetic: none -> 1.41 us  [layer(): jnp.stack(jnp.split(by_block, lax.axis_size('expert'), axis=1))]
    select_n x2, other arithmetic: 1.55 us -> 0.18 us  [layer(): by_block = jnp.take(expert_out, order, axis=1)]
where the time goes in v1:
time: 95.3 us; the launch traced here: 94.4 us
  starting transfers between devices  33.3 us (35%)
  waiting for transfers between devices  30.8 us (32%)
  local copies, waits for them, and re-layouts  12.4 us (13%)
  blocking collectives  8.35 us (9%)
  other arithmetic  4.62 us (5%)
  matrix products  4.43 us (5%)
    ppermute x6, starting transfers between devices, layer(): lax.ppermute(outgoing[:, s], AXES, expert_pairs(p, s, False))  12.4 us
    ppermute x4, waiting for transfers between devices, per_device(): parts.append(lax.ppermute(cols, AXES, pairs))  11 us
    all_to_all x1, blocking collectives, layer(): gathered = lax.all_to_all(spread, 'dp', 0, 0, tiled=True)  8.35 us
    all_to_all x1, waiting for transfers between devices, layer(): gathered = lax.all_to_all(spread, 'dp', 0, 0, tiled=True)  7.95 us
    all_to_all x2, waiting for transfers between devices, layer(): lax.all_to_all(jnp.stack(jnp.split(by_block, lax.axis_size('expert'), axi...  7.88 us
    all_to_all x2, starting transfers between devices, layer(): lax.all_to_all(jnp.stack(jnp.split(by_block, lax.axis_size('expert'), axi...  6.8 us
    ppermute x4, starting transfers between devices, per_device(): parts.append(lax.ppermute(cols, AXES, pairs))  5.17 us
    ppermute x3, starting transfers between devices, per_device(): lax.ppermute(down_parts[s], 'dp', [(i, dring.ahead(i, s)) for i in range(...  4.51 us
  transfers between devices with their start and end apart: 16, of which 9 were waited for; matrix products, arithmetic and copies ran while one was open for 10% of the time, Pallas kernels for 0%

profile of v1, /device:TPU:1, one launch (start us, length us, event | category | flops | bytes accessed | tf_op | source)
XLA Modules:
  0.0 94.4 jit_solution(10729555722182896590)
XLA Ops:
  0.0 2.2 %dynamic-slice_bitcast_fusion = (bf16[176,768]{1,0:T(8,128)(2,1)}, bf16[176,768]{1,0:T(8,128)(2,1)}, bf16[176,768]{1,0:T(8,128)(2,1)S(1)}, bf16[176,768]{1,0:T(8,128)(2,1)}) fusion(bf16[1,1,176,3072]{3,2,1,0:T(8,128)(2,1)} %param.15, s32[]{:T(128)S(6)} %select_n.72, s32[]{:T(128)S(6)} %select_n.70, s32[]{:T(128)S(6)} %select_n.69, s32[]{:T(128)S(6)} %select_n.71), kind=kLoop, calls=%fused_computation.33 | loop fusion | bytes 2162704 | tf_op jit(solution)/shard_map/dynamic_slice | solution.py:78
  2.2 2.1 %collective-permute-start.3 = (bf16[176,768]{1,0:T(8,128)(2,1)}, bf16[176,768]{1,0:T(8,128)(2,1)}, u32[]{:S(2)}, u32[]{:S(2)}) collective-permute-start(bf16[176,768]{1,0:T(8,128)(2,1)} %get-tuple-element.14), channel_id=1, source_target_pairs={{0,8},{8,0},{16,24},{24,16},{1,9},{9,1},{17,25},{25,17},{2,10},{10... | collective-permute-start | bytes 811016 | tf_op jit(solution)/shard_map/ppermute | solution.py:82
  4.4 2.3 %collective-permute-start.4 = (bf16[176,768]{1,0:T(8,128)(2,1)}, bf16[176,768]{1,0:T(8,128)(2,1)}, u32[]{:S(2)}, u32[]{:S(2)}) collective-permute-start(bf16[176,768]{1,0:T(8,128)(2,1)} %get-tuple-element.15), channel_id=1, source_target_pairs={{0,16},{8,24},{16,0},{24,8},{1,17},{9,25},{17,1},{25,9},{2,18},{10... | collective-permute-start | bytes 811016 | tf_op jit(solution)/shard_map/ppermute | solution.py:82
  8.2 0.4 convolution_convert_fusion.1
  8.7 0.7 fusion.20
  9.4 1.3 %collective-permute-start = (bf16[2,16,3072]{2,1,0:T(8,128)(2,1)}, bf16[2,16,3072]{2,1,0:T(8,128)(2,1)}, u32[]{:S(2)}, u32[]{:S(2)}) collective-permute-start(bf16[2,16,3072]{2,1,0:T(8,128)(2,1)} %get-tuple-element.35), channel_id=1, source_target_pairs={{0,1},{1,0},{2,3},{3,2},{8,9},{9,8},{10,11},{11,10},{16,17},{17,16... | collective-permute-start | bytes 589832 | tf_op jit(solution)/shard_map/ppermute | solution.py:105
  10.7 1.3 %collective-permute-start.1 = (bf16[2,16,3072]{2,1,0:T(8,128)(2,1)S(1)}, bf16[2,16,3072]{2,1,0:T(8,128)(2,1)}, u32[]{:S(2)}, u32[]{:S(2)}) collective-permute-start(bf16[2,16,3072]{2,1,0:T(8,128)(2,1)S(1)} %get-tuple-element.34), channel_id=1, source_target_pairs={{0,2},{1,3},{2,0},{3,1},{8,10},{9,11},{10,8},{11,9},{16,18},{17,19... | collective-permute-start | bytes 589832 | tf_op jit(solution)/shard_map/ppermute | solution.py:105
  12.1 1.3 %collective-permute-start.2 = (bf16[2,16,3072]{2,1,0:T(8,128)(2,1)S(1)}, bf16[2,16,3072]{2,1,0:T(8,128)(2,1)}, u32[]{:S(2)}, u32[]{:S(2)}) collective-permute-start(bf16[2,16,3072]{2,1,0:T(8,128)(2,1)S(1)} %get-tuple-element.36), channel_id=1, source_target_pairs={{0,3},{1,2},{2,1},{3,0},{8,11},{9,10},{10,9},{11,8},{16,19},{17,18... | collective-permute-start | bytes 589832 | tf_op jit(solution)/shard_map/ppermute | solution.py:105
  13.8 1.3 %multiply_reduce_fusion.1 = (f32[2,4,16]{2,1,0:T(4,128)S(1)}, bf16[2,4,16,3072]{3,2,1,0:T(8,128)(2,1)S(1)}) fusion(bf16[2,1,16,3072]{3,2,1,0:T(8,128)(2,1)} %bitcast.28, bf16[2,1,16,3072]{3,2,1,0:T(8,128)(2,1)} %bitcast.26, bf16[2,1,16,3072]{3,2,1,0:T(8,128)(2,1)} %bitcast.24, bf16[2,1,16,3072]{3,2,1,0:T(8,128)(2,1)S(1)} %get-tuple-element.33), kind=kLoop, calls=%fused_computation.8 | loop fusion | flops 2359168 | bytes 1573376 | tf_op jit(solution)/shard_map/reduce_sum | solution.py:107
  15.2 0.4 convolution_multiply_fusion.3
  15.7 0.8 copy-done.1
  16.5 0.5 fusion.6
  17.0 0.7 broadcast_in_dim.85
  17.6 4.5 %all-to-all-start = ((bf16[4,128,176]{1,2,0:T(8,128)(2,1)}), bf16[4,128,176]{1,2,0:T(8,128)(2,1)S(1)}, u32[]{:S(2)}, u32[]{:S(2)}) async-start(bf16[4,128,176]{1,2,0:T(8,128)(2,1)} %broadcast_in_dim.85), calls=%async_computation | async-start | bytes 360448 | tf_op jit(solution)/shard_map/all_to_all | solution.py:114
  22.1 1.0 %constant_dynamic-update-slice_fusion.2 = bf16[704,768]{1,0:T(8,128)(2,1)S(1)} fusion(bf16[704,768]{1,0:T(8,128)(2,1)S(1)} %constant_dynamic-update-slice_fusion.3, bf16[176,768]{1,0:T(8,128)(2,1)} %collective-permute-done.3), kind=kLoop, calls=%fused_computation.75 | loop fusion | bytes 540672
  23.1 1.0 %constant_dynamic-update-slice_fusion.1 = bf16[704,768]{1,0:T(8,128)(2,1)S(1)} fusion(bf16[704,768]{1,0:T(8,128)(2,1)S(1)} %constant_dynamic-update-slice_fusion.2, bf16[176,768]{1,0:T(8,128)(2,1)} %collective-permute-done.4), kind=kLoop, calls=%fused_computation.74 | loop fusion | bytes 540672
  24.1 1.0 %constant_dynamic-update-slice_fusion = bf16[704,768]{1,0:T(8,128)(2,1)S(1)} fusion(bf16[704,768]{1,0:T(8,128)(2,1)S(1)} %constant_dynamic-update-slice_fusion.1, bf16[176,768]{1,0:T(8,128)(2,1)} %collective-permute-done.5), kind=kLoop, calls=%fused_computation.73 | loop fusion | bytes 540672 | tf_op jit(solution)/shard_map/concatenate | solution.py:85
  25.1 7.9 %all-to-all-done = bf16[4,128,176]{1,2,0:T(8,128)(2,1)S(1)} async-done(((bf16[4,128,176]{1,2,0:T(8,128)(2,1)}), bf16[4,128,176]{1,2,0:T(8,128)(2,1)S(1)}, u32[]{:S(2)}, u32[]{:S(2)}) %all-to-all-start) | async-done | bytes 180256 | tf_op jit(solution)/shard_map/all_to_all | solution.py:114
  33.0 0.6 gather_fusion.1
  34.1 0.6 gather_fusion.2
  34.8 0.7 pad_maximum_fusion.3
  35.5 3.4 %all-to-all-start.1 = ((bf16[4,2,1,16,768]{4,3,1,2,0:T(8,128)(2,1)}), bf16[4,2,1,16,768]{4,3,1,2,0:T(8,128)(2,1)S(1)}, u32[]{:S(2)}, u32[]{:S(2)}) async-start(bf16[4,2,1,16,768]{4,3,1,2,0:T(8,128)(2,1)} %pad_maximum_fusion.3), calls=%async_computation.1 | async-start | bytes 393216 | tf_op jit(solution)/shard_map/all_to_all | solution.py:128
  39.1 3.9 %all-to-all-done.1 = bf16[4,2,1,16,768]{4,3,1,2,0:T(8,128)(2,1)S(1)} async-done(((bf16[4,2,1,16,768]{4,3,1,2,0:T(8,128)(2,1)}), bf16[4,2,1,16,768]{4,3,1,2,0:T(8,128)(2,1)S(1)}, u32[]{:S(2)}, u32[]{:S(2)}) %all-to-all-start.1) | async-done | bytes 196640 | tf_op jit(solution)/shard_map/all_to_all | solution.py:128
  43.2 1.3 %collective-permute-start.6 = (bf16[2,24,768]{2,1,0:T(8,128)(2,1)S(1)}, bf16[2,24,768]{2,1,0:T(8,128)(2,1)S(1)}, u32[]{:S(2)}, u32[]{:S(2)}) collective-permute-start(bf16[2,24,768]{2,1,0:T(8,128)(2,1)S(1)} %fusion), channel_id=1, source_target_pairs={{0,4},{1,5},{2,6},{3,7},{8,12},{9,13},{10,14},{11,15},{16,20},{17,... | collective-permute-start | bytes 221192 | tf_op jit(solution)/shard_map/ppermute | solution.py:162
  44.5 1.3 %collective-permute-start.7 = (bf16[2,24,768]{2,1,0:T(8,128)(2,1)S(1)}, bf16[2,24,768]{2,1,0:T(8,128)(2,1)S(1)}, u32[]{:S(2)}, u32[]{:S(2)}) collective-permute-start(bf16[2,24,768]{2,1,0:T(8,128)(2,1)S(1)} %fusion), channel_id=1, source_target_pairs={{0,12},{1,13},{2,14},{3,15},{8,4},{9,5},{10,6},{11,7},{16,28},{17,... | collective-permute-start | bytes 221192 | tf_op jit(solution)/shard_map/ppermute | solution.py:162
  45.8 1.3 %collective-permute-start.8 = (bf16[2,24,768]{2,1,0:T(8,128)(2,1)S(1)}, bf16[2,24,768]{2,1,0:T(8,128)(2,1)S(1)}, u32[]{:S(2)}, u32[]{:S(2)}) collective-permute-start(bf16[2,24,768]{2,1,0:T(8,128)(2,1)S(1)} %fusion), channel_id=1, source_target_pairs={{0,20},{1,21},{2,22},{3,23},{8,28},{9,29},{10,30},{11,31},{16,4},{... | collective-permute-start | bytes 221192 | tf_op jit(solution)/shard_map/ppermute | solution.py:162
  47.1 1.3 %collective-permute-start.9 = (bf16[2,24,768]{2,1,0:T(8,128)(2,1)S(1)}, bf16[2,24,768]{2,1,0:T(8,128)(2,1)S(1)}, u32[]{:S(2)}, u32[]{:S(2)}) collective-permute-start(bf16[2,24,768]{2,1,0:T(8,128)(2,1)S(1)} %fusion), channel_id=1, source_target_pairs={{0,28},{1,29},{2,30},{3,31},{8,20},{9,21},{10,22},{11,23},{16,12},... | collective-permute-start | bytes 221192 | tf_op jit(solution)/shard_map/ppermute | solution.py:162
  48.4 4.2 %collective-permute-done.6 = bf16[2,24,768]{2,1,0:T(8,128)(2,1)S(1)} collective-permute-done((bf16[2,24,768]{2,1,0:T(8,128)(2,1)S(1)}, bf16[2,24,768]{2,1,0:T(8,128)(2,1)S(1)}, u32[]{:S(2)}, u32[]{:S(2)}) %collective-permute-start.6) | collective-permute-done | bytes 73760 | tf_op jit(solution)/shard_map/ppermute | solution.py:162
  52.6 3.6 %collective-permute-done.7 = bf16[2,24,768]{2,1,0:T(8,128)(2,1)S(1)} collective-permute-done((bf16[2,24,768]{2,1,0:T(8,128)(2,1)S(1)}, bf16[2,24,768]{2,1,0:T(8,128)(2,1)S(1)}, u32[]{:S(2)}, u32[]{:S(2)}) %collective-permute-start.7) | collective-permute-done | bytes 73760 | tf_op jit(solution)/shard_map/ppermute | solution.py:162
  56.3 0.8 collective-permute-done.8
  57.1 2.3 %collective-permute-done.9 = bf16[2,24,768]{2,1,0:T(8,128)(2,1)S(1)} collective-permute-done((bf16[2,24,768]{2,1,0:T(8,128)(2,1)S(1)}, bf16[2,24,768]{2,1,0:T(8,128)(2,1)S(1)}, u32[]{:S(2)}, u32[]{:S(2)}) %collective-permute-start.9) | collective-permute-done | bytes 73760 | tf_op jit(solution)/shard_map/ppermute | solution.py:162
  59.4 0.6 gather_fusion
  60.1 0.4 convolution_convert_fusion
  60.6 2.7 %collective-permute-start.10 = (bf16[2,16,3072]{2,1,0:T(8,128)(2,1)S(1)}, bf16[2,16,3072]{2,1,0:T(8,128)(2,1)S(1)}, u32[]{:S(2)}, u32[]{:S(2)}) collective-permute-start(bf16[2,16,3072]{2,1,0:T(8,128)(2,1)S(1)} %get-tuple-element.31), channel_id=1, source_target_pairs={{4,5},{5,4},{6,7},{7,6},{12,13},{13,12},{14,15},{15,14},{20,21},{2... | collective-permute-start | bytes 589832 | tf_op jit(solution)/shard_map/ppermute | solution.py:105
  63.4 2.2 %collective-permute-start.11 = (bf16[2,16,3072]{2,1,0:T(8,128)(2,1)S(1)}, bf16[2,16,3072]{2,1,0:T(8,128)(2,1)S(1)}, u32[]{:S(2)}, u32[]{:S(2)}) collective-permute-start(bf16[2,16,3072]{2,1,0:T(8,128)(2,1)S(1)} %get-tuple-element.30), channel_id=1, source_target_pairs={{4,6},{5,7},{6,4},{7,5},{12,14},{13,15},{14,12},{15,13},{20,22},{2... | collective-permute-start | bytes 589832 | tf_op jit(solution)/shard_map/ppermute | solution.py:105
  65.5 3.5 %collective-permute-start.12 = (bf16[2,16,3072]{2,1,0:T(8,128)(2,1)S(1)}, bf16[2,16,3072]{2,1,0:T(8,128)(2,1)S(1)}, u32[]{:S(2)}, u32[]{:S(2)}) collective-permute-start(bf16[2,16,3072]{2,1,0:T(8,128)(2,1)S(1)} %get-tuple-element.32), channel_id=1, source_target_pairs={{4,7},{5,6},{6,5},{7,4},{12,15},{13,14},{14,13},{15,12},{20,23},{2... | collective-permute-start | bytes 589832 | tf_op jit(solution)/shard_map/ppermute | solution.py:105
  69.0 1.0 %collective-permute-done.11 = bf16[2,16,3072]{2,1,0:T(8,128)(2,1)S(1)} collective-permute-done((bf16[2,16,3072]{2,1,0:T(8,128)(2,1)S(1)}, bf16[2,16,3072]{2,1,0:T(8,128)(2,1)S(1)}, u32[]{:S(2)}, u32[]{:S(2)}) %collective-permute-start.11) | collective-permute-done | bytes 196640 | tf_op jit(solution)/shard_map/ppermute | solution.py:105
  70.1 2.9 %collective-permute-done.12 = bf16[2,16,3072]{2,1,0:T(8,128)(2,1)S(1)} collective-permute-done((bf16[2,16,3072]{2,1,0:T(8,128)(2,1)S(1)}, bf16[2,16,3072]{2,1,0:T(8,128)(2,1)S(1)}, u32[]{:S(2)}, u32[]{:S(2)}) %collective-permute-start.12) | collective-permute-done | bytes 196640 | tf_op jit(solution)/shard_map/ppermute | solution.py:105
  73.4 0.5 convolution_multiply_fusion.1
  73.8 0.8 copy-done.2
  74.6 0.5 fusion.7
  75.1 8.3 %all_to_all.20 = bf16[4,128,176]{1,2,0:T(8,128)(2,1)S(1)} all-to-all(bf16[4,128,176]{1,2,0:T(8,128)(2,1)S(1)} %broadcast_in_dim.87), channel_id=1, replica_groups=mesh['dp'=4,'pipe'=2,'expert'=4] {'dp'}, dimensions={0} | all-to-all | bytes 360448 | tf_op jit(solution)/shard_map/all_to_all | solution.py:114
  83.5 0.7 gather_fusion.3
  84.6 0.7 gather_fusion.4
  85.5 0.7 pad_maximum_fusion.4
  86.2 3.4 %all-to-all-start.3 = ((bf16[4,2,1,16,768]{4,3,1,2,0:T(8,128)(2,1)}), bf16[4,2,1,16,768]{4,3,1,2,0:T(8,128)(2,1)S(1)}, u32[]{:S(2)}, u32[]{:S(2)}) async-start(bf16[4,2,1,16,768]{4,3,1,2,0:T(8,128)(2,1)} %pad_maximum_fusion.4), calls=%async_computation.3 | async-start | bytes 393216 | tf_op jit(solution)/shard_map/all_to_all | solution.py:128
  89.5 4.0 %all-to-all-done.3 = bf16[4,2,1,16,768]{4,3,1,2,0:T(8,128)(2,1)S(1)} async-done(((bf16[4,2,1,16,768]{4,3,1,2,0:T(8,128)(2,1)}), bf16[4,2,1,16,768]{4,3,1,2,0:T(8,128)(2,1)S(1)}, u32[]{:S(2)}, u32[]{:S(2)}) %all-to-all-start.3) | async-done | bytes 196640 | tf_op jit(solution)/shard_map/all_to_all | solution.py:128
  93.6 0.9 fusion.5
  (79 shorter events, 4.0 us)
Async XLA Ops:
  0.0 15.2 %copy-start = (bf16[1,1,3072,176]{2,3,1,0:T(8,128)(2,1)S(1)}, bf16[1,1,3072,176]{2,3,1,0:T(8,128)(2,1)}, u32[]{:S(2)}) copy-start(bf16[1,1,3072,176]{2,3,1,0:T(8,128)(2,1)} %param.13) | copy-start | bytes 3244036
  0.0 6.7 %copy-start.4 = (s32[1,2,24,2]{2,3,1,0:T(2,128)S(1)}, s32[1,2,24,2]{2,3,1,0:T(2,128)}, u32[]{:S(2)}) copy-start(s32[1,2,24,2]{2,3,1,0:T(2,128)} %param.11) | copy-start | bytes 1156
  0.0 8.2 %copy-start.3 = (bf16[2,24,3072]{2,1,0:T(8,128)(2,1)S(1)}, bf16[2,24,3072]{2,1,0:T(8,128)(2,1)}, u32[]{:S(2)}) copy-start(bf16[2,24,3072]{2,1,0:T(8,128)(2,1)} %param.10) | copy-start | bytes 884740
  2.2 19.9 %collective-permute-start.3 = (bf16[176,768]{1,0:T(8,128)(2,1)}, bf16[176,768]{1,0:T(8,128)(2,1)}, u32[]{:S(2)}, u32[]{:S(2)}) collective-permute-start(bf16[176,768]{1,0:T(8,128)(2,1)} %get-tuple-element.14), channel_id=1, source_target_pairs={{0,8},{8,0},{16,24},{24,16},{1,9},{9,1},{17,25},{25,17},{2,10},{10... | collective-permute-start | bytes 811016 | tf_op jit(solution)/shard_map/ppermute | solution.py:82
  4.4 18.8 %collective-permute-start.4 = (bf16[176,768]{1,0:T(8,128)(2,1)}, bf16[176,768]{1,0:T(8,128)(2,1)}, u32[]{:S(2)}, u32[]{:S(2)}) collective-permute-start(bf16[176,768]{1,0:T(8,128)(2,1)} %get-tuple-element.15), channel_id=1, source_target_pairs={{0,16},{8,24},{16,0},{24,8},{1,17},{9,25},{17,1},{25,9},{2,18},{10... | collective-permute-start | bytes 811016 | tf_op jit(solution)/shard_map/ppermute | solution.py:82
  8.6 5.0 %copy-start.12 = (f32[1,2,24,2]{2,3,1,0:T(2,128)S(1)}, f32[1,2,24,2]{2,3,1,0:T(2,128)}, u32[]{:S(2)}) copy-start(f32[1,2,24,2]{2,3,1,0:T(2,128)} %param.12) | copy-start | bytes 1156
  9.4 4.3 %collective-permute-start = (bf16[2,16,3072]{2,1,0:T(8,128)(2,1)}, bf16[2,16,3072]{2,1,0:T(8,128)(2,1)}, u32[]{:S(2)}, u32[]{:S(2)}) collective-permute-start(bf16[2,16,3072]{2,1,0:T(8,128)(2,1)} %get-tuple-element.35), channel_id=1, source_target_pairs={{0,1},{1,0},{2,3},{3,2},{8,9},{9,8},{10,11},{11,10},{16,17},{17,16... | collective-permute-start | bytes 589832 | tf_op jit(solution)/shard_map/ppermute | solution.py:105
  10.7 3.0 %collective-permute-start.1 = (bf16[2,16,3072]{2,1,0:T(8,128)(2,1)S(1)}, bf16[2,16,3072]{2,1,0:T(8,128)(2,1)}, u32[]{:S(2)}, u32[]{:S(2)}) collective-permute-start(bf16[2,16,3072]{2,1,0:T(8,128)(2,1)S(1)} %get-tuple-element.34), channel_id=1, source_target_pairs={{0,2},{1,3},{2,0},{3,1},{8,10},{9,11},{10,8},{11,9},{16,18},{17,19... | collective-permute-start | bytes 589832 | tf_op jit(solution)/shard_map/ppermute | solution.py:105
  12.1 1.7 %collective-permute-start.2 = (bf16[2,16,3072]{2,1,0:T(8,128)(2,1)S(1)}, bf16[2,16,3072]{2,1,0:T(8,128)(2,1)}, u32[]{:S(2)}, u32[]{:S(2)}) collective-permute-start(bf16[2,16,3072]{2,1,0:T(8,128)(2,1)S(1)} %get-tuple-element.36), channel_id=1, source_target_pairs={{0,3},{1,2},{2,1},{3,0},{8,11},{9,10},{10,9},{11,8},{16,19},{17,18... | collective-permute-start | bytes 589832 | tf_op jit(solution)/shard_map/ppermute | solution.py:105
  13.5 20.1 %copy-start.5 = (pred[4]{0:T(512)(128)(4,1)}, pred[4]{0:T(512)(128)(4,1)S(1)}, u32[]{:S(2)}) copy-start(pred[4]{0:T(512)(128)(4,1)S(1)} %get-tuple-element.21) | copy-start | bytes 16
  13.5 19.5 %copy-start.8 = (s32[1024]{0:T(1024)}, s32[1024]{0:T(1024)S(1)}, u32[]{:S(2)}) copy-start(s32[1024]{0:T(1024)S(1)} %pad_clamp_fusion.2) | copy-start | bytes 12292
  13.6 21.1 %copy-start.10 = (pred[4]{0:T(512)(128)(4,1)}, pred[4]{0:T(512)(128)(4,1)S(1)}, u32[]{:S(2)}) copy-start(pred[4]{0:T(512)(128)(4,1)S(1)} %get-tuple-element.19) | copy-start | bytes 16
  13.6 20.5 %copy-start.9 = (s32[1024]{0:T(1024)}, s32[1024]{0:T(1024)S(1)}, u32[]{:S(2)}) copy-start(s32[1024]{0:T(1024)S(1)} %pad_clamp_fusion.1) | copy-start | bytes 12292
  13.7 10.4 %collective-permute-start.5 = (bf16[176,768]{1,0:T(8,128)(2,1)}, bf16[176,768]{1,0:T(8,128)(2,1)}, u32[]{:S(2)}, u32[]{:S(2)}) collective-permute-start(bf16[176,768]{1,0:T(8,128)(2,1)} %get-tuple-element.16), channel_id=1, source_target_pairs={{0,24},{8,16},{16,8},{24,0},{1,25},{9,17},{17,9},{25,1},{2,26},{10... | collective-permute-start | bytes 811016 | tf_op jit(solution)/shard_map/ppermute | solution.py:82
  15.2 1.3 %copy-start.1 = (bf16[1,1,3072,176]{2,3,1,0:T(8,128)(2,1)S(1)}, bf16[1,1,3072,176]{2,3,1,0:T(8,128)(2,1)}, u32[]{:S(2)}) copy-start(bf16[1,1,3072,176]{2,3,1,0:T(8,128)(2,1)} %param.14) | copy-start | bytes 3244036
  17.6 15.4 %all-to-all-start = ((bf16[4,128,176]{1,2,0:T(8,128)(2,1)}), bf16[4,128,176]{1,2,0:T(8,128)(2,1)S(1)}, u32[]{:S(2)}, u32[]{:S(2)}) async-start(bf16[4,128,176]{1,2,0:T(8,128)(2,1)} %broadcast_in_dim.85), calls=%async_computation | async-start | bytes 360448 | tf_op jit(solution)/shard_map/all_to_all | solution.py:114
  35.5 7.5 %all-to-all-start.1 = ((bf16[4,2,1,16,768]{4,3,1,2,0:T(8,128)(2,1)}), bf16[4,2,1,16,768]{4,3,1,2,0:T(8,128)(2,1)S(1)}, u32[]{:S(2)}, u32[]{:S(2)}) async-start(bf16[4,2,1,16,768]{4,3,1,2,0:T(8,128)(2,1)} %pad_maximum_fusion.3), calls=%async_computation.1 | async-start | bytes 393216 | tf_op jit(solution)/shard_map/all_to_all | solution.py:128
  38.9 21.1 %copy-start.6 = (pred[4]{0:T(512)(128)(4,1)S(1)}, pred[4]{0:T(512)(128)(4,1)}, u32[]{:S(2)}) copy-start(pred[4]{0:T(512)(128)(4,1)} %copy-done.5) | copy-start | bytes 16
  43.2 9.4 %collective-permute-start.6 = (bf16[2,24,768]{2,1,0:T(8,128)(2,1)S(1)}, bf16[2,24,768]{2,1,0:T(8,128)(2,1)S(1)}, u32[]{:S(2)}, u32[]{:S(2)}) collective-permute-start(bf16[2,24,768]{2,1,0:T(8,128)(2,1)S(1)} %fusion), channel_id=1, source_target_pairs={{0,4},{1,5},{2,6},{3,7},{8,12},{9,13},{10,14},{11,15},{16,20},{17,... | collective-permute-start | bytes 221192 | tf_op jit(solution)/shard_map/ppermute | solution.py:162
  44.5 11.7 %collective-permute-start.7 = (bf16[2,24,768]{2,1,0:T(8,128)(2,1)S(1)}, bf16[2,24,768]{2,1,0:T(8,128)(2,1)S(1)}, u32[]{:S(2)}, u32[]{:S(2)}) collective-permute-start(bf16[2,24,768]{2,1,0:T(8,128)(2,1)S(1)} %fusion), channel_id=1, source_target_pairs={{0,12},{1,13},{2,14},{3,15},{8,4},{9,5},{10,6},{11,7},{16,28},{17,... | collective-permute-start | bytes 221192 | tf_op jit(solution)/shard_map/ppermute | solution.py:162
  45.8 11.3 %collective-permute-start.8 = (bf16[2,24,768]{2,1,0:T(8,128)(2,1)S(1)}, bf16[2,24,768]{2,1,0:T(8,128)(2,1)S(1)}, u32[]{:S(2)}, u32[]{:S(2)}) collective-permute-start(bf16[2,24,768]{2,1,0:T(8,128)(2,1)S(1)} %fusion), channel_id=1, source_target_pairs={{0,20},{1,21},{2,22},{3,23},{8,28},{9,29},{10,30},{11,31},{16,4},{... | collective-permute-start | bytes 221192 | tf_op jit(solution)/shard_map/ppermute | solution.py:162
  47.1 12.3 %collective-permute-start.9 = (bf16[2,24,768]{2,1,0:T(8,128)(2,1)S(1)}, bf16[2,24,768]{2,1,0:T(8,128)(2,1)S(1)}, u32[]{:S(2)}, u32[]{:S(2)}) collective-permute-start(bf16[2,24,768]{2,1,0:T(8,128)(2,1)S(1)} %fusion), channel_id=1, source_target_pairs={{0,28},{1,29},{2,30},{3,31},{8,20},{9,21},{10,22},{11,23},{16,12},... | collective-permute-start | bytes 221192 | tf_op jit(solution)/shard_map/ppermute | solution.py:162
  60.6 8.4 %collective-permute-start.10 = (bf16[2,16,3072]{2,1,0:T(8,128)(2,1)S(1)}, bf16[2,16,3072]{2,1,0:T(8,128)(2,1)S(1)}, u32[]{:S(2)}, u32[]{:S(2)}) collective-permute-start(bf16[2,16,3072]{2,1,0:T(8,128)(2,1)S(1)} %get-tuple-element.31), channel_id=1, source_target_pairs={{4,5},{5,4},{6,7},{7,6},{12,13},{13,12},{14,15},{15,14},{20,21},{2... | collective-permute-start | bytes 589832 | tf_op jit(solution)/shard_map/ppermute | solution.py:105
  63.4 6.7 %collective-permute-start.11 = (bf16[2,16,3072]{2,1,0:T(8,128)(2,1)S(1)}, bf16[2,16,3072]{2,1,0:T(8,128)(2,1)S(1)}, u32[]{:S(2)}, u32[]{:S(2)}) collective-permute-start(bf16[2,16,3072]{2,1,0:T(8,128)(2,1)S(1)} %get-tuple-element.30), channel_id=1, source_target_pairs={{4,6},{5,7},{6,4},{7,5},{12,14},{13,15},{14,12},{15,13},{20,22},{2... | collective-permute-start | bytes 589832 | tf_op jit(solution)/shard_map/ppermute | solution.py:105
  65.5 7.5 %collective-permute-start.12 = (bf16[2,16,3072]{2,1,0:T(8,128)(2,1)S(1)}, bf16[2,16,3072]{2,1,0:T(8,128)(2,1)S(1)}, u32[]{:S(2)}, u32[]{:S(2)}) collective-permute-start(bf16[2,16,3072]{2,1,0:T(8,128)(2,1)S(1)} %get-tuple-element.32), channel_id=1, source_target_pairs={{4,7},{5,6},{6,5},{7,4},{12,15},{13,14},{14,13},{15,12},{20,23},{2... | collective-permute-start | bytes 589832 | tf_op jit(solution)/shard_map/ppermute | solution.py:105
  73.3 1.3 %copy-start.2 = (bf16[1,1,3072,176]{2,3,1,0:T(8,128)(2,1)S(1)}, bf16[1,1,3072,176]{2,3,1,0:T(8,128)(2,1)}, u32[]{:S(2)}) copy-start(bf16[1,1,3072,176]{2,3,1,0:T(8,128)(2,1)} %param.14) | copy-start | bytes 3244036
  74.6 9.6 %copy-start.7 = (pred[4]{0:T(512)(128)(4,1)S(1)}, pred[4]{0:T(512)(128)(4,1)}, u32[]{:S(2)}) copy-start(pred[4]{0:T(512)(128)(4,1)} %copy-done.5) | copy-start | bytes 16
  84.2 1.1 %copy-start.11 = (pred[4]{0:T(512)(128)(4,1)S(1)}, pred[4]{0:T(512)(128)(4,1)}, u32[]{:S(2)}) copy-start(pred[4]{0:T(512)(128)(4,1)} %copy-done.10) | copy-start | bytes 16
  86.2 7.4 %all-to-all-start.3 = ((bf16[4,2,1,16,768]{4,3,1,2,0:T(8,128)(2,1)}), bf16[4,2,1,16,768]{4,3,1,2,0:T(8,128)(2,1)S(1)}, u32[]{:S(2)}, u32[]{:S(2)}) async-start(bf16[4,2,1,16,768]{4,3,1,2,0:T(8,128)(2,1)} %pad_maximum_fusion.4), calls=%async_computation.3 | async-start | bytes 393216 | tf_op jit(solution)/shard_map/all_to_all | solution.py:128
